TPU v7x, 256 devices: a whole 4x4x8 slice. The times are simulated.
256 devices in a mesh: dp: 8 (over x, core), expert: 32 (over y, z).
Axes of the slice: x: 4, y: 4, z: 8, core: 2. Of those that a mesh axis runs over, the one named last changes fastest.
Arguments:
- tokens: bfloat16 [12288, 2048], P(('dp', 'expert')), may hold values from -6 to 6
- routes: int32 [12288, 6], P(('dp', 'expert')), may hold values from 0 to 31, all different within a row; in each aligned block of 48 rows (0 to 47, 48 to 95, ...) at most 12 rows name the same one
- gates: float32 [12288, 6], P(('dp', 'expert')), may hold values from 0.02 to 0.5
- cotangent: bfloat16 [12288, 2048], P(('dp', 'expert')), may hold values from -6 to 6
- swap_flag: int32 [32], replicated, may hold values from 0 to 1, as said below
- w_up: bfloat16 [32, 2048, 1408], P('expert', 'dp'), may hold values from -0.125 to 0.125
- w_down: bfloat16 [32, 1408, 2048], P('expert', 'dp'), may hold values from -0.15625 to 0.15625
- m_up: bfloat16 [32, 2048, 1408], P('expert', 'dp'), may hold values from -12 to 12
- v_up: bfloat16 [32, 2048, 1408], P('expert', 'dp'), may hold values from 1 to 50
- m_down: bfloat16 [32, 1408, 2048], P('expert', 'dp'), may hold values from -12 to 12
- v_down: bfloat16 [32, 1408, 2048], P('expert', 'dp'), may hold values from 1 to 50
Outputs:
- mixed: bfloat16 [12288, 2048], P(('dp', 'expert'))
- input_grad: bfloat16 [12288, 2048], P(('dp', 'expert'))
- new_w_up: bfloat16 [32, 2048, 1408], P('expert', 'dp')
- new_w_down: bfloat16 [32, 1408, 2048], P('expert', 'dp')
- new_m_up: bfloat16 [32, 2048, 1408], P('expert', 'dp')
- new_v_up: bfloat16 [32, 2048, 1408], P('expert', 'dp')
- new_m_down: bfloat16 [32, 1408, 2048], P('expert', 'dp')
- new_v_down: bfloat16 [32, 1408, 2048], P('expert', 'dp')
Inputs may be any that keep to these rules, and one draw needn't show every extreme that they name: `routes`: in each aligned block of 48 rows (the tokens of one device) no expert is chosen by more than 12 rows, a bound that some block reaches; the 6 experts of a row differ. swap_flag[e] == swap_flag[e xor 1] for every e; the pairs of experts 0 and 2 * (8) trade places in every draw, and some other pair stays.
All inputs are finite; a program needn't handle non-finite values.
Results may differ from a plain program's by a relative error of at most 0.015.
Values may be sent and summed in bfloat16 or wider, within the bound.
No kernel may reach another device: no remote copies, remote signals or barrier semaphores. Data moves between devices by JAX's collectives and lax.ppermute only.
A program may use at most 128 MiB of HBM per device.

v0:
```python
import jax
import jax.numpy as jnp
from jax import lax
from jax.sharding import PartitionSpec as P

ADAM_STEP = 10
beta_one = 0.9
beta_two = 0.95
learn_rate = 0.001
adam_eps = 1e-08


def partner(value, axis, distance):
    mask = 2**distance
    pairs = [(source, source ^ mask) for source in range(lax.axis_size(axis))]
    return lax.ppermute(value, axis, pairs)


def silu_slope(value):
    sigma = jax.nn.sigmoid(value)
    return sigma * (1.0 + value * (1.0 - sigma))


def adam_update(weight, first_moment, second_moment, gradient):
    first_new = beta_one * first_moment.astype(jnp.float32) + (1.0 - beta_one) * gradient
    second_new = (
        beta_two * second_moment.astype(jnp.float32) + (1.0 - beta_two) * gradient * gradient
    )
    correct_one = 1.0 - beta_one**ADAM_STEP
    correct_two = 1.0 - beta_two**ADAM_STEP
    weight_new = weight.astype(jnp.float32) - learn_rate * (first_new / correct_one) / (
        jnp.sqrt(second_new / correct_two) + adam_eps
    )
    return (
        weight_new.astype(jnp.bfloat16),
        first_new.astype(jnp.bfloat16),
        second_new.astype(jnp.bfloat16),
    )


def contract_rows(left, right):
    return lax.dot_general(
        left, right, (((0,), (0,)), ((), ())), preferred_element_type=jnp.float32
    )


def contract_cols(left, right):
    return lax.dot_general(
        left, right, (((1,), (1,)), ((), ())), preferred_element_type=jnp.float32
    )


def stack_state(members):
    return jnp.stack([member.reshape(-1) for member in members])


def unstack_state(stacked, member_shapes):
    return tuple(
        (stacked[number].reshape(member_shape) for number, member_shape in enumerate(member_shapes))
    )


def body(tokens, routes, gates, cotangent, swap_flag, w_up, w_down, m_up, v_up, m_down, v_down):
    experts = lax.axis_size("expert")
    my_slot = lax.axis_index("expert")
    tok_count, model_width = tokens.shape
    chosen = routes.shape[1]
    pair_count = tok_count * chosen
    capacity = pair_count * 4 // (3 * experts)
    row_total = experts * capacity
    my_flag = swap_flag[my_slot]
    swapped = my_flag == 1
    w_up_in = partner(w_up, "expert", 0)
    w_down_in = partner(w_down, "expert", 0)
    up_moments = partner(jnp.concatenate([m_up, v_up], axis=0), "expert", 0)
    down_moments = partner(jnp.concatenate([m_down, v_down], axis=0), "expert", 0)
    w_up_use = jnp.where(swapped, w_up_in, w_up)
    w_down_use = jnp.where(swapped, w_down_in, w_down)
    m_up_use = jnp.where(swapped, up_moments[0:1], m_up)
    v_up_use = jnp.where(swapped, up_moments[1:2], v_up)
    m_down_use = jnp.where(swapped, down_moments[0:1], m_down)
    v_down_use = jnp.where(swapped, down_moments[1:2], v_down)
    flat_routes = routes.reshape(pair_count)
    dest_routes = jnp.bitwise_xor(flat_routes, swap_flag[flat_routes])
    one_hot = (dest_routes[:, None] == jnp.arange(experts, dtype=jnp.int32)[None, :]).astype(
        jnp.int32
    )
    position = jnp.sum(jnp.cumsum(one_hot, axis=0) * one_hot, axis=1) - 1
    slot_index = dest_routes * capacity + position
    source = (
        jnp.full((row_total,), -1, jnp.int32)
        .at[slot_index]
        .set(jnp.arange(pair_count, dtype=jnp.int32))
    )
    is_live = source >= 0
    safe_source = jnp.maximum(source, 0)
    token_ids = safe_source // chosen
    send_tokens = jnp.where(
        is_live[:, None], tokens[token_ids], jnp.zeros((), jnp.bfloat16)
    ).reshape(experts, capacity, model_width)
    live_gates = jnp.where(is_live, gates.reshape(pair_count)[safe_source], 0.0)
    send_grads = (
        (live_gates[:, None] * cotangent[token_ids].astype(jnp.float32))
        .astype(jnp.bfloat16)
        .reshape(experts, capacity, model_width)
    )
    up_full = lax.all_gather(w_up_use, "dp", axis=1, tiled=True)[0]
    down_full = lax.all_gather(w_down_use, "dp", axis=1, tiled=True)[0]
    got_both = lax.all_to_all(
        jnp.concatenate([send_tokens, send_grads], axis=1),
        "expert",
        split_axis=0,
        concat_axis=0,
        tiled=True,
    )
    expert_rows = got_both[:, :capacity].reshape(row_total, model_width)
    grad_rows = got_both[:, capacity:].reshape(row_total, model_width)
    up_act = jnp.dot(expert_rows, up_full, preferred_element_type=jnp.float32)
    hidden = jax.nn.silu(up_act).astype(jnp.bfloat16)
    expert_out = jnp.dot(hidden, down_full, preferred_element_type=jnp.float32).astype(jnp.bfloat16)
    returned = lax.all_to_all(
        expert_out.reshape(experts, capacity, model_width),
        "expert",
        split_axis=0,
        concat_axis=0,
        tiled=True,
    )
    picked = returned.reshape(row_total, model_width)[slot_index].reshape(
        tok_count, chosen, model_width
    )
    mixed = jnp.sum(gates[:, :, None] * picked.astype(jnp.float32), axis=1).astype(jnp.bfloat16)
    hidden_grad = contract_cols(grad_rows, down_full)
    up_grad = (hidden_grad * silu_slope(up_act)).astype(jnp.bfloat16)
    input_part = contract_cols(up_grad, up_full).astype(jnp.bfloat16)
    back_grads = lax.all_to_all(
        input_part.reshape(experts, capacity, model_width),
        "expert",
        split_axis=0,
        concat_axis=0,
        tiled=True,
    )
    picked_grad = back_grads.reshape(row_total, model_width)[slot_index].reshape(
        tok_count, chosen, model_width
    )
    input_grad = jnp.sum(picked_grad.astype(jnp.float32), axis=1).astype(jnp.bfloat16)
    up_gradient = lax.psum_scatter(
        contract_rows(expert_rows, up_grad).astype(jnp.bfloat16),
        "dp",
        scatter_dimension=0,
        tiled=True,
    ).astype(jnp.float32)
    down_gradient = lax.psum_scatter(
        contract_rows(hidden, grad_rows).astype(jnp.bfloat16), "dp", scatter_dimension=0, tiled=True
    ).astype(jnp.float32)
    up_new = adam_update(w_up_use[0], m_up_use[0], v_up_use[0], up_gradient)
    down_new = adam_update(w_down_use[0], m_down_use[0], v_down_use[0], down_gradient)
    return (
        mixed,
        input_grad,
        up_new[0][None],
        down_new[0][None],
        up_new[1][None],
        up_new[2][None],
        down_new[1][None],
        down_new[2][None],
    )


def solution(mesh):
    return jax.shard_map(
        body,
        mesh=mesh,
        in_specs=(
            P(("dp", "expert"), None),
            P(("dp", "expert"), None),
            P(("dp", "expert"), None),
            P(("dp", "expert"), None),
            P(),
            P("expert", "dp", None),
            P("expert", "dp", None),
            P("expert", "dp", None),
            P("expert", "dp", None),
            P("expert", "dp", None),
            P("expert", "dp", None),
        ),
        out_specs=(
            P(("dp", "expert"), None),
            P(("dp", "expert"), None),
            P("expert", "dp", None),
            P("expert", "dp", None),
            P("expert", "dp", None),
            P("expert", "dp", None),
            P("expert", "dp", None),
            P("expert", "dp", None),
        ),
        check_vma=False,
    )
```

profile of v0, /device:TPU:8, one launch (start us, length us, event | category | flops | bytes accessed | tf_op | source)
XLA Modules:
  0.0 443.3 jit_solution(2398692835408480219)
XLA Ops:
  7.2 2.0 collective-permute-start
  10.1 2.0 fusion.44
  12.8 1.9 fusion.45
  14.7 4.3 fusion.38
  19.0 6.6 %collective-permute-done = bf16[1,256,1408]{2,1,0:T(8,128)(2,1)S(1)} collective-permute-done((bf16[1,256,1408]{2,1,0:T(8,128)(2,1)}, bf16[1,256,1408]{2,1,0:T(8,128)(2,1)S(1)}, u32[]{:S(2)}, u32[]{:S(2)}) %collective-permute-start) | collective-permute-done | bytes 720928 | tf_op jit(solution)/shard_map/ppermute | solution.py:16
  25.6 2.1 broadcast_select_fusion.2
  28.2 15.6 %fusion.42 = (s32[288]{0:T(512)S(1)}, s32[288]{0:T(512)S(1)}) fusion(s32[288]{0:T(512)S(1)} %reshape.168, pred[288]{0:T(512)(128)(4,1)S(1)} %get-tuple-element.32, pred[288]{0:T(512)(128)(4,1)S(1)} %get-tuple-element.31, pred[288]{0:T(512)(128)(4,1)S(1)} %get-tuple-element.30, pred[288]{0:T(512)(128)(4,1)S(1)} %get-tuple-element.29, ...), kind=kLoop, calls=%fused_computation.115 | loop fusion | flops 7488 | bytes 11908 | tf_op jit(solution)/shard_map/xor | solution.py:84
  45.2 2.9 scatter_custom_fusion
  48.1 2.8 gather_fusion.1
  51.2 3.1 gather_fusion.2
  54.3 3.2 gather_fusion
  57.5 2.4 gather.25
  59.9 3.9 reshape.180
  64.0 2.0 copy-done.3
  67.4 81.6 %all_to_all.15 = bf16[32,24,2048]{2,1,0:T(8,128)(2,1)S(1)} all-to-all(bf16[32,24,2048]{2,1,0:T(8,128)(2,1)S(1)} %pad_maximum_fusion), channel_id=1, replica_groups=mesh['dp'=8,'expert'=32] {'expert'}, dimensions={0} | all-to-all | bytes 6291456 | tf_op jit(solution)/shard_map/all_to_all | solution.py:109
  149.0 2.3 fusion.43
  151.3 3.6 reshape.172
  154.9 1.4 reshape.175
  156.3 5.8 %fusion.6 = f32[384,1408]{1,0:T(8,128)S(1)} fusion(bf16[384,2048]{1,0:T(8,128)(2,1)} %reshape.172, bf16[1,2048,1408]{2,1,0:T(8,128)(2,1)} %all-gather.3.cloned.1.call-done), kind=kOutput, calls=%fused_computation.14 | convolution fusion | flops 2214592512 | bytes 9502720 | tf_op jit(solution)/shard_map/dot_general | solution.py:118
  162.2 1.4 copy-done.15
  163.5 5.1 %convolution_convert_fusion = bf16[1408,2048]{1,0:T(8,128)(2,1)} fusion(bf16[384,2048]{1,0:T(8,128)(2,1)S(1)} %copy-done.9, f32[384,1408]{1,0:T(8,128)S(1)} %fusion.6), kind=kOutput, calls=%fused_computation.6 | convolution fusion | flops 2220179456 | bytes 9502720 | tf_op jit(solution)/shard_map/dot_general | solution.py:42
  170.1 3.0 collective-permute-start.3
  174.0 43.8 %collective-permute-done.1 = bf16[1,176,2048]{2,1,0:T(8,128)(2,1)S(1)} collective-permute-done((bf16[1,176,2048]{2,1,0:T(8,128)(2,1)S(1)}, bf16[1,176,2048]{2,1,0:T(8,128)(2,1)S(1)}, u32[]{:S(2)}, u32[]{:S(2)}) %collective-permute-start.1) | collective-permute-done | bytes 720928 | tf_op jit(solution)/shard_map/ppermute | solution.py:16
  218.6 5.2 %fusion.35 = (bf16[1,176,2048]{2,1,0:T(8,128)(2,1)}, bf16[1,176,2048]{2,1,0:T(8,128)(2,1)}, bf16[1,176,2048]{2,1,0:T(8,128)(2,1)}, bf16[1,176,2048]{2,1,0:T(8,128)(2,1)}) fusion(bf16[176,2048]{1,0:T(8,128)(2,1)} %reduce-scatter.5.cloned.1.call-done, bf16[1,176,2048]{2,1,0:T(8,128)(2,1)S(1)} %copy-done.6, bf16[2,176,2048]{2,1,0:T(8,128)(2,1)} %collective-permute-done.3, ...), kind=kLoop, calls=%fused_computation.55 | loop fusion | flops 7929856 | bytes 7929857 | tf_op jit(solution)/shard_map/broadcast_in_dim | solution.py:161
  224.0 40.1 %all-gather.5.cloned.1.call-done = bf16[1,1408,2048]{2,1,0:T(8,128)(2,1)} async-done(((bf16[1,176,2048]{2,1,0:T(8,128)(2,1)}), bf16[1,1408,2048]{2,1,0:T(8,128)(2,1)}) %all-gather.5.cloned.1.call-update) | async-done | bytes 5767184 | tf_op jit(solution)/shard_map/all_gather | solution.py:108
  264.2 7.2 %fusion.11 = bf16[384,1408]{1,0:T(8,128)(2,1)S(1)} fusion(bf16[384,2048]{1,0:T(8,128)(2,1)S(1)} %copy-done.9, bf16[1,1408,2048]{2,1,0:T(8,128)(2,1)} %all-gather.5.cloned.1.call-done, f32[384,1408]{1,0:T(8,128)} %copy-done.15), kind=kOutput, calls=%fused_computation.20 | convolution fusion | flops 2219458560 | bytes 10584064 | tf_op jit(solution)/shard_map/dot_general | solution.py:48
  272.3 5.1 %convolution_convert_fusion.1 = bf16[2048,1408]{1,0:T(8,128)(2,1)} fusion(bf16[384,2048]{1,0:T(8,128)(2,1)S(1)} %copy-done.8, bf16[384,1408]{1,0:T(8,128)(2,1)S(1)} %fusion.11), kind=kOutput, calls=%fused_computation.7 | convolution fusion | flops 2217476096 | bytes 8421376 | tf_op jit(solution)/shard_map/dot_general | solution.py:42
  278.7 5.3 %fusion.14 = bf16[384,2048]{1,0:T(8,128)(2,1)S(1)} fusion(bf16[384,1408]{1,0:T(8,128)(2,1)S(1)} %copy-done.14, bf16[1,2048,1408]{2,1,0:T(8,128)(2,1)} %all-gather.3.cloned.1.call-done), kind=kOutput, calls=%fused_computation.21 | convolution fusion | flops 2215378944 | bytes 8421376 | tf_op jit(solution)/shard_map/dot_general | solution.py:48
  284.0 1.6 reshape.176
  285.6 10.2 %all-to-all-start.2 = ((bf16[32,12,2048]{2,1,0:T(8,128)(2,1)}), bf16[32,12,2048]{2,1,0:T(8,128)(2,1)S(1)}, u32[]{:S(2)}, u32[]{:S(2)}) async-start(bf16[32,12,2048]{2,1,0:T(8,128)(2,1)} %reshape.176), calls=%async_computation.2 | async-start | bytes 4194304 | tf_op jit(solution)/shard_map/all_to_all | solution.py:135
  295.7 7.3 %fusion.17 = bf16[384,2048]{1,0:T(8,128)(2,1)} fusion(bf16[1,1408,2048]{2,1,0:T(8,128)(2,1)} %all-gather.5.cloned.1.call-done, f32[384,1408]{1,0:T(8,128)} %copy-done.15), kind=kOutput, calls=%fused_computation.22 | convolution fusion | flops 2218082304 | bytes 9502720 | tf_op jit(solution)/shard_map/dot_general | solution.py:120
  303.0 3.7 reshape.173
  306.6 37.0 %all-to-all-done.2 = bf16[32,12,2048]{2,1,0:T(8,128)(2,1)S(1)} async-done(((bf16[32,12,2048]{2,1,0:T(8,128)(2,1)}), bf16[32,12,2048]{2,1,0:T(8,128)(2,1)S(1)}, u32[]{:S(2)}, u32[]{:S(2)}) %all-to-all-start.2) | async-done | bytes 1572896 | tf_op jit(solution)/shard_map/all_to_all | solution.py:135
  343.6 1.3 copy-done.4
  345.0 9.0 %all-to-all-start.1 = ((bf16[32,12,2048]{2,1,0:T(8,128)(2,1)}), bf16[32,12,2048]{2,1,0:T(8,128)(2,1)}, u32[]{:S(2)}, u32[]{:S(2)}) async-start(bf16[32,12,2048]{2,1,0:T(8,128)(2,1)} %reshape.173), calls=%async_computation.1 | async-start | bytes 4194304 | tf_op jit(solution)/shard_map/all_to_all | solution.py:121
  354.0 2.4 pad_maximum_fusion.1
  356.3 1.5 collective-permute-start.2
  357.8 2.5 reshape.177
  360.3 2.4 gather_fusion.4
  362.8 1.4 reshape.178
  364.1 40.4 %all-to-all-done.1 = bf16[32,12,2048]{2,1,0:T(8,128)(2,1)} async-done(((bf16[32,12,2048]{2,1,0:T(8,128)(2,1)}), bf16[32,12,2048]{2,1,0:T(8,128)(2,1)}, u32[]{:S(2)}, u32[]{:S(2)}) %all-to-all-start.1) | async-done | bytes 1572896 | tf_op jit(solution)/shard_map/all_to_all | solution.py:121
  404.5 2.5 reshape.174
  407.0 3.0 gather_fusion.3
  410.0 2.2 reshape.181
  412.2 3.1 reduce_sum.32
  415.2 1.8 multiply_reduce_fusion
  417.1 14.6 %collective-permute-done.2 = bf16[2,256,1408]{2,1,0:T(8,128)(2,1)} collective-permute-done((bf16[2,256,1408]{2,1,0:T(8,128)(2,1)}, bf16[2,256,1408]{2,1,0:T(8,128)(2,1)}, u32[]{:S(2)}, u32[]{:S(2)}) %collective-permute-start.2) | collective-permute-done | bytes 1441824 | tf_op jit(solution)/shard_map/ppermute | solution.py:16
  431.6 5.2 %fusion.30 = (bf16[1,256,1408]{2,1,0:T(8,128)(2,1)}, bf16[1,256,1408]{2,1,0:T(8,128)(2,1)}, bf16[1,256,1408]{2,1,0:T(8,128)(2,1)}) fusion(bf16[256,1408]{1,0:T(8,128)(2,1)} %reduce-scatter.3.cloned.1.call-done, bf16[1,256,1408]{2,1,0:T(8,128)(2,1)} %param.19, bf16[2,256,1408]{2,1,0:T(8,128)(2,1)} %collective-permute-done.2, pred[]{:T(512)} %bitcast.33, ...), kind=kLoop, calls=%fused_computation.44 | loop fusion | flops 7569408 | bytes 6488065 | tf_op jit(solution)/shard_map/broadcast_in_dim | solution.py:163
  (68 shorter events, 10.3 us)
Async XLA Ops:
  7.2 44.0 %copy-start = (bf16[48,2048]{1,0:T(8,128)(2,1)S(1)}, bf16[48,2048]{1,0:T(8,128)(2,1)}, u32[]{:S(2)}) copy-start(bf16[48,2048]{1,0:T(8,128)(2,1)} %param.14) | copy-start | bytes 589828
  7.2 20.8 %copy-start.12 = (f32[48,6]{0,1:T(8,128)S(1)}, f32[48,6]{0,1:T(8,128)}, u32[]{:S(2)}) copy-start(f32[48,6]{0,1:T(8,128)} %param.13) | copy-start | bytes 3460
  7.2 149.1 %all-gather.3.cloned.1.call-start = ((), (), s32[]{:S(2)}) async-start(), calls=%async_computation.5 | async-start | bytes 6488064 | tf_op jit(solution)/shard_map/all_gather | solution.py:107
  7.2 18.4 %collective-permute-start = (bf16[1,256,1408]{2,1,0:T(8,128)(2,1)}, bf16[1,256,1408]{2,1,0:T(8,128)(2,1)S(1)}, u32[]{:S(2)}, u32[]{:S(2)}) collective-permute-start(bf16[1,256,1408]{2,1,0:T(8,128)(2,1)} %param.16), channel_id=1, source_target_pairs={{0,1},{1,0},{2,3},{3,2},{4,5},{5,4},{6,7},{7,6},{8,9},{9,8},{10,11... | collective-permute-start | bytes 2162696 | tf_op jit(solution)/shard_map/ppermute | solution.py:16
  27.7 190.9 %reduce-scatter.5.cloned.1.call-start = ((), (), s32[]{:S(2)}) async-start(), calls=%async_computation.8 | async-start | bytes 6488064 | tf_op jit(solution)/shard_map/reduce_scatter | solution.py:152
  51.2 3.1 copy-start.2
  63.8 2.2 copy-start.3
  156.3 7.2 %copy-start.9 = (bf16[384,2048]{1,0:T(8,128)(2,1)S(1)}, bf16[384,2048]{1,0:T(8,128)(2,1)}, u32[]{:S(2)}) copy-start(bf16[384,2048]{1,0:T(8,128)(2,1)} %reshape.175) | copy-start | bytes 4718596
  162.1 1.4 copy-start.15
  168.7 1.1 copy-start.6
  168.7 1.3 copy-start.7
  168.7 95.5 %all-gather.5.cloned.1.call-start = ((), (), s32[]{:S(2)}) async-start(), calls=%async_computation.6 | async-start | bytes 6488064 | tf_op jit(solution)/shard_map/all_gather | solution.py:108
  170.0 3.1 copy-start.10
  170.1 48.5 %collective-permute-start.3 = (bf16[2,176,2048]{2,1,0:T(8,128)(2,1)S(1)}, bf16[2,176,2048]{2,1,0:T(8,128)(2,1)}, u32[]{:S(2)}, u32[]{:S(2)}) collective-permute-start(bf16[2,176,2048]{2,1,0:T(8,128)(2,1)S(1)} %pad_maximum_fusion.2), channel_id=1, source_target_pairs={{0,1},{1,0},{2,3},{3,2},{4,5},{5,4},{6,7},{7,6},{8,9},{9,8},{10,11... | collective-permute-start | bytes 4325384 | tf_op jit(solution)/shard_map/ppermute | solution.py:16
  173.1 44.6 %collective-permute-start.1 = (bf16[1,176,2048]{2,1,0:T(8,128)(2,1)S(1)}, bf16[1,176,2048]{2,1,0:T(8,128)(2,1)S(1)}, u32[]{:S(2)}, u32[]{:S(2)}) collective-permute-start(bf16[1,176,2048]{2,1,0:T(8,128)(2,1)S(1)} %copy-done.10), channel_id=1, source_target_pairs={{0,1},{1,0},{2,3},{3,2},{4,5},{5,4},{6,7},{7,6},{8,9},{9,8},{10,11... | collective-permute-start | bytes 2162696 | tf_op jit(solution)/shard_map/ppermute | solution.py:16
  217.7 0.9 copy-start.11
  223.8 48.6 %copy-start.8 = (bf16[384,2048]{1,0:T(8,128)(2,1)S(1)}, bf16[384,2048]{1,0:T(8,128)(2,1)}, u32[]{:S(2)}) copy-start(bf16[384,2048]{1,0:T(8,128)(2,1)} %reshape.172) | copy-start | bytes 4718596
  223.8 207.8 %reduce-scatter.3.cloned.1.call-start = ((), (), s32[]{:S(2)}) async-start(), calls=%async_computation.7 | async-start | bytes 6488064 | tf_op jit(solution)/shard_map/reduce_scatter | solution.py:146
  271.3 1.0 copy-start.13
  277.5 1.2 copy-start.14
  285.6 58.1 %all-to-all-start.2 = ((bf16[32,12,2048]{2,1,0:T(8,128)(2,1)}), bf16[32,12,2048]{2,1,0:T(8,128)(2,1)S(1)}, u32[]{:S(2)}, u32[]{:S(2)}) async-start(bf16[32,12,2048]{2,1,0:T(8,128)(2,1)} %reshape.176), calls=%async_computation.2 | async-start | bytes 4194304 | tf_op jit(solution)/shard_map/all_to_all | solution.py:135
  306.6 47.3 %copy-start.5 = (bf16[1,256,1408]{2,1,0:T(8,128)(2,1)S(1)}, bf16[1,256,1408]{2,1,0:T(8,128)(2,1)}, u32[]{:S(2)}) copy-start(bf16[1,256,1408]{2,1,0:T(8,128)(2,1)} %param.19) | copy-start | bytes 2162692
  343.6 1.3 copy-start.4
  345.0 59.5 %all-to-all-start.1 = ((bf16[32,12,2048]{2,1,0:T(8,128)(2,1)}), bf16[32,12,2048]{2,1,0:T(8,128)(2,1)}, u32[]{:S(2)}, u32[]{:S(2)}) async-start(bf16[32,12,2048]{2,1,0:T(8,128)(2,1)} %reshape.173), calls=%async_computation.1 | async-start | bytes 4194304 | tf_op jit(solution)/shard_map/all_to_all | solution.py:121
  356.3 75.3 %collective-permute-start.2 = (bf16[2,256,1408]{2,1,0:T(8,128)(2,1)}, bf16[2,256,1408]{2,1,0:T(8,128)(2,1)}, u32[]{:S(2)}, u32[]{:S(2)}) collective-permute-start(bf16[2,256,1408]{2,1,0:T(8,128)(2,1)} %pad_maximum_fusion.1), channel_id=1, source_target_pairs={{0,1},{1,0},{2,3},{3,2},{4,5},{5,4},{6,7},{7,6},{8,9},{9,8},{10,11... | collective-permute-start | bytes 4325384 | tf_op jit(solution)/shard_map/ppermute | solution.py:16
  431.6 5.2 %copy-start.1 = (bf16[48,2048]{1,0:T(8,128)(2,1)S(1)}, bf16[48,2048]{1,0:T(8,128)(2,1)}, u32[]{:S(2)}) copy-start(bf16[48,2048]{1,0:T(8,128)(2,1)} %param.14) | copy-start | bytes 589828
Sparse Core Ops, SparseCore 0:
  27.8 43.7 all-gather.2
  168.8 42.1 reduce-scatter.4
  223.9 40.2 all-gather.4
  277.6 44.1 reduce-scatter.2
where the time goes:
time: 445 us; the launch traced here: 443 us
  waiting for transfers between devices  182 us (41%)
  blocking collectives  81.6 us (18%)
  local copies, waits for them, and re-layouts  59.5 us (13%)
  other arithmetic  42.5 us (10%)
  matrix products  35.7 us (8%)
  starting transfers between devices  26.8 us (6%)
  between operations  14.7 us (3%)
    all_to_all x1, blocking collectives, body(): lax.all_to_all(jnp.concatenate([send_tokens, send_grads], axis=1), 'exper...  81.6 us
    ppermute x4, waiting for transfers between devices, partner(): return lax.ppermute(value, axis, pairs)  64.9 us
    all_to_all x1, waiting for transfers between devices, body(): lax.all_to_all(expert_out.reshape(experts, capacity, model_width), 'exper...  40.4 us
    all_gather x1, waiting for transfers between devices, body(): down_full = lax.all_gather(w_down_use, 'dp', axis=1, tiled=True)[0]  40.1 us
    all_to_all x1, waiting for transfers between devices, body(): lax.all_to_all(input_part.reshape(experts, capacity, model_width), 'exper...  37 us
    xor x1, other arithmetic, body(): dest_routes = jnp.bitwise_xor(flat_routes, swap_flag[flat_routes])  15.6 us
    dot_general x2, matrix products, contract_cols(): lax.dot_general(left, right, (((1,), (1,)), ((), ())), preferred_element_...  12.4 us
    dot_general x2, matrix products, contract_rows(): lax.dot_general(left, right, (((0,), (0,)), ((), ())), preferred_element_...  10.2 us
  transfers between devices with their start and end apart: 10, of which 6 were waited for; matrix products, arithmetic and copies ran while one was open for 21% of the time, Pallas kernels for 0%

commit v1 on v0

--- a/solution.py
+++ b/solution.py
@@ -8,6 +8,13 @@
 beta_two = 0.95
 learn_rate = 0.001
 adam_eps = 1e-08
+
+
+def gather_over(x, axis, d):
+    n_dev = lax.axis_size(axis)
+    tiles = jnp.stack([x for _ in range(n_dev)])
+    tiles = lax.all_to_all(tiles, axis, split_axis=0, concat_axis=0)
+    return jnp.concatenate(tiles, axis=d)
 
 
 def partner(value, axis, distance):
@@ -105,7 +112,7 @@
         .reshape(experts, capacity, model_width)
     )
     up_full = lax.all_gather(w_up_use, "dp", axis=1, tiled=True)[0]
-    down_full = lax.all_gather(w_down_use, "dp", axis=1, tiled=True)[0]
+    down_full = gather_over(w_down_use, "dp", 1)[0]
     got_both = lax.all_to_all(
         jnp.concatenate([send_tokens, send_grads], axis=1),
         "expert",

time: 445 us -> 466 us (1.047)
  blocking collectives: 81.6 us -> 153 us
  waiting for transfers between devices: 182 us -> 141 us
    all_to_all x0 -> x1, blocking collectives: none -> 71.6 us  [gather_over(): tiles = lax.all_to_all(tiles, axis, split_axis=0, concat_axis=0)]
    all_gather x1 -> x0, waiting for transfers between devices: 40.1 us -> none  [body(): down_full = lax.all_gather(w_down_use, 'dp', axis=1, tiled=True)[0]]
    unnamed x34 -> x38, local copies, waits for them, and re-layouts: 10 us -> 9.96 us
  transfers between devices with their start and end apart: 10 -> 9, of which waited for: 6 -> 5; matrix products, arithmetic and copies ran while one was open for 21% -> 20% of each run, Pallas kernels for 0% -> 0%
where the time goes in v1:
time: 466 us; the launch traced here: 464 us
  blocking collectives  153 us (33%)
  waiting for transfers between devices  141 us (30%)
  local copies, waits for them, and re-layouts  57.9 us (12%)
  other arithmetic  41.7 us (9%)
  matrix products  31.4 us (7%)
  starting transfers between devices  24.2 us (5%)
  between operations  14.7 us (3%)
    all_to_all x1, blocking collectives, body(): lax.all_to_all(jnp.concatenate([send_tokens, send_grads], axis=1), 'exper...  81.6 us
    all_to_all x1, blocking collectives, gather_over(): tiles = lax.all_to_all(tiles, axis, split_axis=0, concat_axis=0)  71.6 us
    ppermute x4, waiting for transfers between devices, partner(): return lax.ppermute(value, axis, pairs)  64.4 us
    all_to_all x1, waiting for transfers between devices, body(): lax.all_to_all(expert_out.reshape(experts, capacity, model_width), 'exper...  40.4 us
    all_to_all x1, waiting for transfers between devices, body(): lax.all_to_all(input_part.reshape(experts, capacity, model_width), 'exper...  36.2 us
    xor x1, other arithmetic, body(): dest_routes = jnp.bitwise_xor(flat_routes, swap_flag[flat_routes])  15.6 us
    dot_general x2, matrix products, contract_rows(): lax.dot_general(left, right, (((0,), (0,)), ((), ())), preferred_element_...  10.2 us
    unnamed x38, local copies, waits for them, and re-layouts  9.96 us
  transfers between devices with their start and end apart: 9, of which 5 were waited for; matrix products, arithmetic and copies ran while one was open for 20% of the time, Pallas kernels for 0%

profile of v1, /device:TPU:8, one launch (start us, length us, event | category | flops | bytes accessed | tf_op | source)
XLA Modules:
  0.0 464.4 jit_solution(4760176438642734340)
XLA Ops:
  7.2 2.0 collective-permute-start
  10.1 2.0 fusion.31
  12.8 1.9 fusion.32
  14.7 4.3 fusion.25
  19.0 6.6 %collective-permute-done = bf16[1,256,1408]{2,1,0:T(8,128)(2,1)S(1)} collective-permute-done((bf16[1,256,1408]{2,1,0:T(8,128)(2,1)}, bf16[1,256,1408]{2,1,0:T(8,128)(2,1)S(1)}, u32[]{:S(2)}, u32[]{:S(2)}) %collective-permute-start) | collective-permute-done | bytes 720928 | tf_op jit(solution)/shard_map/ppermute | solution.py:23
  25.6 2.0 broadcast_select_fusion.1
  28.0 15.6 %fusion.29 = (s32[288]{0:T(512)S(1)}, s32[288]{0:T(512)S(1)}) fusion(s32[288]{0:T(512)S(1)} %reshape.169, pred[288]{0:T(512)(128)(4,1)S(1)} %get-tuple-element.32, pred[288]{0:T(512)(128)(4,1)S(1)} %get-tuple-element.31, pred[288]{0:T(512)(128)(4,1)S(1)} %get-tuple-element.30, pred[288]{0:T(512)(128)(4,1)S(1)} %get-tuple-element.29, ...), kind=kLoop, calls=%fused_computation.110 | loop fusion | flops 7488 | bytes 11908 | tf_op jit(solution)/shard_map/xor | solution.py:91
  44.9 2.9 scatter_custom_fusion
  47.9 2.5 gather_fusion.2
  50.3 2.2 reshape.181
  52.8 2.8 gather_fusion.1
  55.7 3.1 gather_fusion
  58.9 2.4 gather.25
  61.6 2.0 copy-done.3
  65.0 81.6 %all_to_all.20 = bf16[32,24,2048]{2,1,0:T(8,128)(2,1)S(1)} all-to-all(bf16[32,24,2048]{2,1,0:T(8,128)(2,1)S(1)} %pad_maximum_fusion), channel_id=1, replica_groups=mesh['dp'=8,'expert'=32] {'expert'}, dimensions={0} | all-to-all | bytes 6291456 | tf_op jit(solution)/shard_map/all_to_all | solution.py:116
  146.6 2.3 fusion.30
  148.9 3.6 reshape.173
  152.6 1.4 reshape.176
  154.0 5.8 %fusion.2 = f32[384,1408]{1,0:T(8,128)S(1)} fusion(bf16[384,2048]{1,0:T(8,128)(2,1)} %reshape.173, bf16[1,2048,1408]{2,1,0:T(8,128)(2,1)} %all-gather.2.cloned.1.call-done), kind=kOutput, calls=%fused_computation.10 | convolution fusion | flops 2214592512 | bytes 9502720 | tf_op jit(solution)/shard_map/dot_general | solution.py:125
  159.8 1.4 copy-done.16
  161.2 5.1 %convolution_convert_fusion = bf16[1408,2048]{1,0:T(8,128)(2,1)} fusion(bf16[384,2048]{1,0:T(8,128)(2,1)S(1)} %copy-done.10, f32[384,1408]{1,0:T(8,128)S(1)} %fusion.2), kind=kOutput, calls=%fused_computation.6 | convolution fusion | flops 2220179456 | bytes 9502720 | tf_op jit(solution)/shard_map/dot_general | solution.py:49
  167.8 3.0 collective-permute-start.3
  171.6 43.8 %collective-permute-done.1 = bf16[1,176,2048]{2,1,0:T(8,128)(2,1)S(1)} collective-permute-done((bf16[1,176,2048]{2,1,0:T(8,128)(2,1)S(1)}, bf16[1,176,2048]{2,1,0:T(8,128)(2,1)S(1)}, u32[]{:S(2)}, u32[]{:S(2)}) %collective-permute-start.1) | collective-permute-done | bytes 720928 | tf_op jit(solution)/shard_map/ppermute | solution.py:23
  216.3 4.5 fusion.21
  221.5 71.6 %all_to_all.21 = bf16[8,1,176,2048]{3,2,1,0:T(8,128)(2,1)S(1)} all-to-all(bf16[8,1,176,2048]{3,2,1,0:T(8,128)(2,1)S(1)} %stack.2), channel_id=1, replica_groups=mesh['dp'=8,'expert'=32] {'dp'}, dimensions={0} | all-to-all | bytes 11534336 | tf_op jit(solution)/shard_map/all_to_all | solution.py:16
  293.1 2.9 fusion.4
  297.0 5.1 %convolution_convert_fusion.1 = bf16[2048,1408]{1,0:T(8,128)(2,1)} fusion(bf16[384,2048]{1,0:T(8,128)(2,1)S(1)} %copy-done.9, bf16[384,1408]{1,0:T(8,128)(2,1)S(1)} %fusion.4), kind=kOutput, calls=%fused_computation.7 | convolution fusion | flops 2217476096 | bytes 8421376 | tf_op jit(solution)/shard_map/dot_general | solution.py:49
  303.3 5.3 %fusion.5 = bf16[384,2048]{1,0:T(8,128)(2,1)S(1)} fusion(bf16[384,1408]{1,0:T(8,128)(2,1)S(1)} %copy-done.15, bf16[1,2048,1408]{2,1,0:T(8,128)(2,1)} %all-gather.2.cloned.1.call-done), kind=kOutput, calls=%fused_computation.17 | convolution fusion | flops 2215378944 | bytes 8421376 | tf_op jit(solution)/shard_map/dot_general | solution.py:55
  308.6 1.6 reshape.177
  310.2 8.1 %all-to-all-start.3 = ((bf16[32,12,2048]{2,1,0:T(8,128)(2,1)}), bf16[32,12,2048]{2,1,0:T(8,128)(2,1)S(1)}, u32[]{:S(2)}, u32[]{:S(2)}) async-start(bf16[32,12,2048]{2,1,0:T(8,128)(2,1)} %reshape.177), calls=%async_computation.3 | async-start | bytes 4194304 | tf_op jit(solution)/shard_map/all_to_all | solution.py:142
  318.3 7.3 %convolution_convert_fusion.2 = bf16[384,2048]{1,0:T(8,128)(2,1)} fusion(bf16[1408,2048]{1,0:T(8,128)(2,1)} %bitcast.123, f32[384,1408]{1,0:T(8,128)} %copy-done.16), kind=kOutput, calls=%fused_computation.18 | convolution fusion | flops 2218082304 | bytes 9502720 | tf_op jit(solution)/shard_map/dot_general | solution.py:127
  325.5 3.7 reshape.174
  329.2 36.2 %all-to-all-done.3 = bf16[32,12,2048]{2,1,0:T(8,128)(2,1)S(1)} async-done(((bf16[32,12,2048]{2,1,0:T(8,128)(2,1)}), bf16[32,12,2048]{2,1,0:T(8,128)(2,1)S(1)}, u32[]{:S(2)}, u32[]{:S(2)}) %all-to-all-start.3) | async-done | bytes 1572896 | tf_op jit(solution)/shard_map/all_to_all | solution.py:142
  365.4 1.3 copy-done.4
  366.8 8.7 %all-to-all-start.2 = ((bf16[32,12,2048]{2,1,0:T(8,128)(2,1)}), bf16[32,12,2048]{2,1,0:T(8,128)(2,1)}, u32[]{:S(2)}, u32[]{:S(2)}) async-start(bf16[32,12,2048]{2,1,0:T(8,128)(2,1)} %reshape.174), calls=%async_computation.2 | async-start | bytes 4194304 | tf_op jit(solution)/shard_map/all_to_all | solution.py:128
  375.5 2.4 pad_maximum_fusion.1
  377.8 1.5 collective-permute-start.2
  379.3 2.5 reshape.178
  381.8 2.4 gather_fusion.4
  384.3 1.4 reshape.179
  385.6 40.4 %all-to-all-done.2 = bf16[32,12,2048]{2,1,0:T(8,128)(2,1)} async-done(((bf16[32,12,2048]{2,1,0:T(8,128)(2,1)}), bf16[32,12,2048]{2,1,0:T(8,128)(2,1)}, u32[]{:S(2)}, u32[]{:S(2)}) %all-to-all-start.2) | async-done | bytes 1572896 | tf_op jit(solution)/shard_map/all_to_all | solution.py:128
  426.0 2.5 reshape.175
  428.5 3.0 gather_fusion.3
  431.5 2.2 reshape.182
  433.6 3.1 reduce_sum.32
  436.7 1.8 multiply_reduce_fusion
  438.5 14.1 %collective-permute-done.2 = bf16[2,256,1408]{2,1,0:T(8,128)(2,1)} collective-permute-done((bf16[2,256,1408]{2,1,0:T(8,128)(2,1)}, bf16[2,256,1408]{2,1,0:T(8,128)(2,1)}, u32[]{:S(2)}, u32[]{:S(2)}) %collective-permute-start.2) | collective-permute-done | bytes 1441824 | tf_op jit(solution)/shard_map/ppermute | solution.py:23
  452.6 5.2 %fusion.17 = (bf16[1,256,1408]{2,1,0:T(8,128)(2,1)}, bf16[1,256,1408]{2,1,0:T(8,128)(2,1)}, bf16[1,256,1408]{2,1,0:T(8,128)(2,1)}) fusion(bf16[256,1408]{1,0:T(8,128)(2,1)} %reduce-scatter.3.cloned.1.call-done, bf16[1,256,1408]{2,1,0:T(8,128)(2,1)} %param.19, bf16[2,256,1408]{2,1,0:T(8,128)(2,1)} %collective-permute-done.2, pred[]{:T(512)} %bitcast.33, ...), kind=kLoop, calls=%fused_computation.39 | loop fusion | flops 7569408 | bytes 6488065 | tf_op jit(solution)/shard_map/broadcast_in_dim | solution.py:170
  (71 shorter events, 10.7 us)
Async XLA Ops:
  7.2 40.7 %copy-start = (bf16[48,2048]{1,0:T(8,128)(2,1)S(1)}, bf16[48,2048]{1,0:T(8,128)(2,1)}, u32[]{:S(2)}) copy-start(bf16[48,2048]{1,0:T(8,128)(2,1)} %param.14) | copy-start | bytes 589828
  7.2 146.8 %all-gather.2.cloned.1.call-start = ((), (), s32[]{:S(2)}) async-start(), calls=%async_computation.6 | async-start | bytes 6488064 | tf_op jit(solution)/shard_map/all_gather | solution.py:114
  7.2 18.4 %collective-permute-start = (bf16[1,256,1408]{2,1,0:T(8,128)(2,1)}, bf16[1,256,1408]{2,1,0:T(8,128)(2,1)S(1)}, u32[]{:S(2)}, u32[]{:S(2)}) collective-permute-start(bf16[1,256,1408]{2,1,0:T(8,128)(2,1)} %param.16), channel_id=1, source_target_pairs={{0,1},{1,0},{2,3},{3,2},{4,5},{5,4},{6,7},{7,6},{8,9},{9,8},{10,11... | collective-permute-start | bytes 2162696 | tf_op jit(solution)/shard_map/ppermute | solution.py:23
  27.7 188.6 %reduce-scatter.5.cloned.1.call-start = ((), (), s32[]{:S(2)}) async-start(), calls=%async_computation.8 | async-start | bytes 6488064 | tf_op jit(solution)/shard_map/reduce_scatter | solution.py:159
  50.3 2.3 copy-start.13
  52.6 3.1 copy-start.2
  61.4 2.2 copy-start.3
  154.0 7.2 %copy-start.10 = (bf16[384,2048]{1,0:T(8,128)(2,1)S(1)}, bf16[384,2048]{1,0:T(8,128)(2,1)}, u32[]{:S(2)}) copy-start(bf16[384,2048]{1,0:T(8,128)(2,1)} %reshape.176) | copy-start | bytes 4718596
  159.8 1.4 copy-start.16
  166.3 1.1 copy-start.7
  166.3 1.3 copy-start.8
  166.3 286.3 %reduce-scatter.3.cloned.1.call-start = ((), (), s32[]{:S(2)}) async-start(), calls=%async_computation.7 | async-start | bytes 6488064 | tf_op jit(solution)/shard_map/reduce_scatter | solution.py:153
  167.6 3.1 copy-start.11
  167.8 48.5 %collective-permute-start.3 = (bf16[2,176,2048]{2,1,0:T(8,128)(2,1)S(1)}, bf16[2,176,2048]{2,1,0:T(8,128)(2,1)}, u32[]{:S(2)}, u32[]{:S(2)}) collective-permute-start(bf16[2,176,2048]{2,1,0:T(8,128)(2,1)S(1)} %pad_maximum_fusion.2), channel_id=1, source_target_pairs={{0,1},{1,0},{2,3},{3,2},{4,5},{5,4},{6,7},{7,6},{8,9},{9,8},{10,11... | collective-permute-start | bytes 4325384 | tf_op jit(solution)/shard_map/ppermute | solution.py:23
  170.8 44.6 %collective-permute-start.1 = (bf16[1,176,2048]{2,1,0:T(8,128)(2,1)S(1)}, bf16[1,176,2048]{2,1,0:T(8,128)(2,1)S(1)}, u32[]{:S(2)}, u32[]{:S(2)}) collective-permute-start(bf16[1,176,2048]{2,1,0:T(8,128)(2,1)S(1)} %copy-done.11), channel_id=1, source_target_pairs={{0,1},{1,0},{2,3},{3,2},{4,5},{5,4},{6,7},{7,6},{8,9},{9,8},{10,11... | collective-permute-start | bytes 2162696 | tf_op jit(solution)/shard_map/ppermute | solution.py:23
  215.4 0.9 copy-start.12
  221.4 71.6 %copy-start.17 = (f32[384,1408]{1,0:T(8,128)S(1)}, f32[384,1408]{1,0:T(8,128)}, u32[]{:S(2)}) copy-start(f32[384,1408]{1,0:T(8,128)} %copy-done.16) | copy-start | bytes 6488068
  293.1 2.9 copy-start.5
  293.1 3.9 copy-start.9
  295.9 1.0 copy-start.14
  302.1 1.2 copy-start.15
  310.2 55.2 %all-to-all-start.3 = ((bf16[32,12,2048]{2,1,0:T(8,128)(2,1)}), bf16[32,12,2048]{2,1,0:T(8,128)(2,1)S(1)}, u32[]{:S(2)}, u32[]{:S(2)}) async-start(bf16[32,12,2048]{2,1,0:T(8,128)(2,1)} %reshape.177), calls=%async_computation.3 | async-start | bytes 4194304 | tf_op jit(solution)/shard_map/all_to_all | solution.py:142
  329.2 46.3 %copy-start.6 = (bf16[1,256,1408]{2,1,0:T(8,128)(2,1)S(1)}, bf16[1,256,1408]{2,1,0:T(8,128)(2,1)}, u32[]{:S(2)}) copy-start(bf16[1,256,1408]{2,1,0:T(8,128)(2,1)} %param.19) | copy-start | bytes 2162692
  365.4 1.3 copy-start.4
  366.8 59.2 %all-to-all-start.2 = ((bf16[32,12,2048]{2,1,0:T(8,128)(2,1)}), bf16[32,12,2048]{2,1,0:T(8,128)(2,1)}, u32[]{:S(2)}, u32[]{:S(2)}) async-start(bf16[32,12,2048]{2,1,0:T(8,128)(2,1)} %reshape.174), calls=%async_computation.2 | async-start | bytes 4194304 | tf_op jit(solution)/shard_map/all_to_all | solution.py:128
  377.8 74.8 %collective-permute-start.2 = (bf16[2,256,1408]{2,1,0:T(8,128)(2,1)}, bf16[2,256,1408]{2,1,0:T(8,128)(2,1)}, u32[]{:S(2)}, u32[]{:S(2)}) collective-permute-start(bf16[2,256,1408]{2,1,0:T(8,128)(2,1)} %pad_maximum_fusion.1), channel_id=1, source_target_pairs={{0,1},{1,0},{2,3},{3,2},{4,5},{5,4},{6,7},{7,6},{8,9},{9,8},{10,11... | collective-permute-start | bytes 4325384 | tf_op jit(solution)/shard_map/ppermute | solution.py:23
  452.6 5.2 %copy-start.1 = (bf16[48,2048]{1,0:T(8,128)(2,1)S(1)}, bf16[48,2048]{1,0:T(8,128)(2,1)}, u32[]{:S(2)}) copy-start(bf16[48,2048]{1,0:T(8,128)(2,1)} %param.14) | copy-start | bytes 589828
Sparse Core Ops, SparseCore 0:
  27.8 43.7 all-gather.1
  166.4 42.0 reduce-scatter.4
  302.2 41.3 reduce-scatter.2
